TPU v7x, 32 devices: a whole 2x2x4 slice. The times are simulated.
32 devices in a mesh: groups: 2 (over x), wide: 4 (over y, core), expert: 4 (over z).
Axes of the slice: x: 2, y: 2, z: 4, core: 2. Of those that a mesh axis runs over, the one named last changes fastest.
Arguments:
- prompts: bfloat16 [8, 128, 6144], P(('groups', 'wide'), None, 'expert'), parts along dimension 0, may hold values from -6 to 6
- span_slot_owner: int32 [8], P('groups'), parts along dimension 0, may hold values from 0 to 3, as said below
- row_expert_index: int32 [768, 2], P('groups'), parts along dimension 0, may hold values from 0 to 7, all different within a row
- tile_tenant_index: int32 [6], P('groups'), parts along dimension 0, may hold values from 0 to 7
- tenant_adapter_slot: int32 [16], P('groups'), parts along dimension 0, may hold values from 0 to 7, each once
- router: bfloat16 [6144, 8], replicated, may hold values from -0.078125 to 0.078125
- gate_weight: bfloat16 [2, 6144, 16384], P(None, None, ('wide', 'expert')), may hold values from -0.078125 to 0.078125
- up_weight: bfloat16 [2, 6144, 16384], P(None, None, ('wide', 'expert')), may hold values from -0.078125 to 0.078125
- down_weight: bfloat16 [2, 16384, 6144], P(None, 'wide', 'expert'), may hold values from -0.046875 to 0.046875
- adapter_down_weight: bfloat16 [16, 2, 6144, 64], P(('groups', 'wide'), None, 'expert'), parts along dimension 0, may hold values from -0.078125 to 0.078125
- adapter_up_weight: bfloat16 [16, 2, 64, 16384], P('groups', None, None, ('wide', 'expert')), parts along dimension 0, may hold values from -0.75 to 0.75
Outputs:
- mixed: bfloat16 [768, 6144], P(('groups', 'wide'), 'expert'), parts along dimension 0
There are 2 independent parts, one for each index of `groups`. A program takes and returns all parts, laid end to end along the dimension named above; an argument that names none is the same for every part. Nothing has to cross between parts.
Inputs may be any that keep to these rules, and one draw needn't show every extreme that they name: `span_slot_owner`: a permutation of the slots; span c, for c < 3, is in slot span_slot_owner[c]. `row_expert_index`: each row names two different experts. `tenant_adapter_slot`: a permutation of the slots. `tile_tenant_index`: tenant of rows 128 * i to 128 * i + 127.
All inputs are finite; a program needn't handle non-finite values.
Results may differ from a plain program's by a relative error of at most 0.0051.
Values may be sent and summed in bfloat16 or wider, within the bound.
No kernel may reach another device: no remote copies, remote signals or barrier semaphores. Data moves between devices by JAX's collectives and lax.ppermute only.
A program may use at most 128 MiB of HBM per device.

v0:
```python
import jax
import jax.numpy as jnp
import numpy as np
from jax import lax
from jax.sharding import Mesh
from jax.sharding import PartitionSpec as P

ADAPTER_SCALE = 0.5
WIDE = ("wy", "wc")
GROUP = ("wy", "wc", "expert")


def per_device(
    prompts,
    span_slot_owner,
    row_expert_index,
    tile_tenant_index,
    tenant_adapter_slot,
    router,
    gate_weight,
    up_weight,
    down_weight,
    adapter_down_weight,
    adapter_up_weight,
):
    span = prompts.shape[1]
    quarter = prompts.shape[2]
    tokens = row_expert_index.shape[0]
    nchunk = tokens // span
    window = gate_weight.shape[0]
    core = lax.axis_index("wc")
    cores = lax.axis_size("wc")
    wide_index = lax.axis_index(WIDE)
    slots_q = lax.all_gather(prompts, WIDE, axis=0, tiled=True)
    rows_q = jnp.take(slots_q, span_slot_owner[:nchunk], axis=0).reshape(tokens, quarter)
    half = tokens // cores
    mine_q = lax.dynamic_slice_in_dim(rows_q, core * half, half, 0)
    mine = lax.all_gather(mine_q, "expert", axis=1, tiled=True)
    other = lax.ppermute(mine, "wc", [(i, (i + 1) % cores) for i in range(cores)])
    first = jnp.where(core == 0, mine, other)
    second = jnp.where(core == 0, other, mine)
    input_rows = jnp.concatenate([first, second], axis=0)
    logits = jnp.dot(input_rows, router, preferred_element_type=jnp.float32)
    experts = jnp.arange(router.shape[1], dtype=jnp.int32)
    picked = (row_expert_index[:, :, None] == experts[None, None, :]).astype(jnp.float32)
    chosen = jnp.sum(picked * logits[:, None, :], axis=2)
    first_prob = jax.nn.sigmoid(chosen[:, 0] - chosen[:, 1])
    second_prob = jax.nn.sigmoid(chosen[:, 1] - chosen[:, 0])
    weight = (
        first_prob[:, None] * picked[:, 0, :window] + second_prob[:, None] * picked[:, 1, :window]
    )
    tile_count = tile_tenant_index.shape[0]
    tile_rows = tokens // tile_count
    resident_slots = adapter_down_weight.shape[0]
    tile_slot_index = jnp.take(tenant_adapter_slot, tile_tenant_index)
    owners = tile_slot_index // resident_slots
    local_index = tile_slot_index % resident_slots
    held = jnp.take(adapter_down_weight, local_index, axis=0)
    partial_rank = jnp.einsum(
        "ntd,nedr->nter",
        rows_q.reshape(tile_count, tile_rows, quarter),
        held,
        preferred_element_type=jnp.float32,
    )
    partial_rank = jnp.where(
        (owners == wide_index)[:, None, None, None], partial_rank, jnp.zeros_like(partial_rank)
    )
    lowrank = lax.reduce_precision(lax.psum(partial_rank, GROUP), exponent_bits=8, mantissa_bits=7)
    tile_up = jnp.take(adapter_up_weight, tile_tenant_index, axis=0)
    adapted_hidden = jnp.einsum(
        "nter,nerf->ntef", lowrank, tile_up.astype(jnp.float32), preferred_element_type=jnp.float32
    ).reshape(tokens, window, tile_up.shape[3])
    running = None
    for expert_number in range(window):
        gate_pre = jnp.dot(
            input_rows, gate_weight[expert_number], preferred_element_type=jnp.float32
        )
        up_value = (
            jnp.dot(input_rows, up_weight[expert_number], preferred_element_type=jnp.float32)
            + ADAPTER_SCALE * adapted_hidden[:, expert_number]
        )
        hidden = (weight[:, expert_number, None] * jax.nn.silu(gate_pre) * up_value).astype(
            jnp.bfloat16
        )
        gathered = lax.all_gather(hidden, "expert", axis=1, tiled=True)
        part = jnp.dot(gathered, down_weight[expert_number], preferred_element_type=jnp.float32)
        running = part if running is None else running + part
    mixed_rows = lax.psum_scatter(running, WIDE, scatter_dimension=0, tiled=True)
    return mixed_rows.astype(jnp.bfloat16)


def solution(mesh):
    groups = mesh.shape["groups"]
    wide = mesh.shape["wide"]
    expert = mesh.shape["expert"]
    split = Mesh(
        np.asarray(mesh.devices).reshape(groups, wide // 2, 2, expert),
        ("groups", "wy", "wc", "expert"),
    )
    rows = ("groups", "wy", "wc")
    in_specs = (
        P(rows, None, "expert"),
        P("groups"),
        P("groups", None),
        P("groups"),
        P("groups"),
        P(),
        P(None, None, GROUP),
        P(None, None, GROUP),
        P(None, WIDE, "expert"),
        P(rows, None, "expert", None),
        P("groups", None, None, GROUP),
    )
    out_specs = P(rows, "expert")
    return jax.shard_map(
        per_device, mesh=split, in_specs=in_specs, out_specs=out_specs, check_vma=False
    )
```

profile of v0, /device:TPU:0, one launch (start us, length us, event | category | flops | bytes accessed | tf_op | source)
XLA Modules:
  0.0 382.7 jit_solution(16340851096399354820)
XLA Ops:
  6.5 0.7 all-gather.5.cloned.1.call-update
  7.3 0.7 compare_and_fusion.2
  8.0 0.1 broadcast_bitcast_fusion
  8.1 0.1 dynamic-slice
  8.1 23.2 %all-gather.5.cloned.1.call-done = bf16[4,128,1536]{2,1,0:T(8,128)(2,1)} async-done(((bf16[1,128,1536]{2,1,0:T(8,128)(2,1)}), bf16[4,128,1536]{2,1,0:T(8,128)(2,1)}) %all-gather.5.cloned.1.call-update) | async-done | bytes 1572880 | tf_op jit(solution)/shard_map/all_gather | solution.py:34
  31.3 2.0 gather_fusion
  33.4 1.1 dynamic-slice_select_fusion
  34.6 50.6 %all-gather.7.cloned.1.call-done = bf16[192,6144]{1,0:T(8,128)(2,1)} async-done(((bf16[192,1536]{1,0:T(8,128)(2,1)}), bf16[192,6144]{1,0:T(8,128)(2,1)}) %all-gather.7.cloned.1.call-update) | async-done | bytes 2359312 | tf_op jit(solution)/shard_map/all_gather | solution.py:38
  85.2 0.6 gather_fusion.2
  85.9 1.8 gather_fusion.3
  87.7 0.2 broadcast_select_fusion.2
  87.8 1.1 copy-done.6
  88.9 0.5 fusion.33
  89.5 0.8 broadcast_select_fusion.3
  90.3 0.6 gather_fusion.1
  90.9 88.2 %all-reduce.2.cloned.1.call-done = f32[3,128,2,64]{1,3,2,0:T(8,128)} async-done(((f32[3,128,2,64]{1,3,2,0:T(8,128)}), f32[3,128,2,64]{1,3,2,0:T(8,128)}) %all-reduce.2.cloned.1.call-update) | async-done | bytes 196624 | tf_op jit(solution)/shard_map/psum | solution.py:68
  179.1 1.6 convolution_bitcast_fusion
  180.7 0.4 copy.17
  181.1 1.9 copy-done.7
  183.0 2.0 broadcast_select_fusion.1
  185.0 1.3 fusion.48
  186.4 8.1 %fusion.4 = f32[384,1024]{1,0:T(8,128)S(1)} fusion(bf16[2,6144,1024]{2,1,0:T(8,128)(2,1)} %param.17, bf16[192,6144]{1,0:T(8,128)(2,1)S(1)} %get-tuple-element.16, bf16[192,6144]{1,0:T(8,128)(2,1)S(1)} %get-tuple-element.15), kind=kOutput, calls=%fused_computation.8 | convolution fusion | flops 4841275392 | bytes 18874368 | tf_op jit(solution)/shard_map/dot_general | solution.py:75
  194.6 10.7 %fusion.24 = bf16[384,1024]{1,0:T(8,128)(2,1)} fusion(f32[384,2,1024]{2,0,1:T(8,128)S(1)} %bitcast.66, f32[384,1024]{1,0:T(8,128)S(1)} %fusion.4, bf16[2,6144,1024]{2,1,0:T(8,128)(2,1)} %param.18, f32[384]{0:T(512)S(1)} %get-tuple-element.6, bf16[192,6144]{1,0:T(8,128)(2,1)S(1)} %get-tuple-element.16, bf16[192,6144]{1,0:T(8,128)(2,1)S(1)} %get-tuple-element.15), kind=kOutput, calls=%fused_computation.31 | convolution fusion | flops 4844814336 | bytes 21235200 | tf_op jit(solution)/shard_map/dot_general | solution.py:79
  205.4 0.2 all-gather.9.cloned.1.call-start
  205.6 9.5 %fusion.10 = f32[384,1024]{1,0:T(8,128)S(1)} fusion(bf16[2,6144,1024]{2,1,0:T(8,128)(2,1)} %param.17, bf16[192,6144]{1,0:T(8,128)(2,1)} %copy-done.10, bf16[192,6144]{1,0:T(8,128)(2,1)} %copy-done.8), kind=kOutput, calls=%fused_computation.14 | convolution fusion | flops 4841275392 | bytes 18874368 | tf_op jit(solution)/shard_map/dot_general | solution.py:75
  215.2 10.8 %fusion.28 = bf16[384,1024]{1,0:T(8,128)(2,1)} fusion(f32[384,2,1024]{2,0,1:T(8,128)S(1)} %bitcast.67, f32[384,1024]{1,0:T(8,128)S(1)} %fusion.10, bf16[2,6144,1024]{2,1,0:T(8,128)(2,1)} %param.18, f32[384]{0:T(512)S(1)} %get-tuple-element.5, bf16[192,6144]{1,0:T(8,128)(2,1)S(1)} %copy-done.11, bf16[192,6144]{1,0:T(8,128)(2,1)S(1)} %copy-done.9), kind=kOutput, calls=%fused_computation.36 | convolution fusion | flops 4844814336 | bytes 21235200 | tf_op jit(solution)/shard_map/dot_general | solution.py:79
  226.1 41.9 %all-gather.11.cloned.1.call-done = bf16[384,4096]{1,0:T(8,128)(2,1)} async-done(((bf16[384,1024]{1,0:T(8,128)(2,1)}), bf16[384,4096]{1,0:T(8,128)(2,1)}) %all-gather.11.cloned.1.call-update) | async-done | bytes 3145744 | tf_op jit(solution)/shard_map/all_gather | solution.py:85
  268.0 10.0 %fusion = f32[384,1536]{1,0:T(8,128)} fusion(bf16[384,4096]{1,0:T(8,128)(2,1)} %all-gather.11.cloned.1.call-done, bf16[2,4096,1536]{2,1,0:T(8,128)(2,1)} %param.19), kind=kOutput, calls=%fused_computation.4 | convolution fusion | flops 4831838208 | bytes 18087936 | tf_op jit(solution)/shard_map/dot_general | solution.py:86
  278.0 53.6 %all-gather.9.cloned.1.call-done = bf16[384,4096]{1,0:T(8,128)(2,1)} async-done(((bf16[384,1024]{1,0:T(8,128)(2,1)}), bf16[384,4096]{1,0:T(8,128)(2,1)}) %all-gather.9.cloned.1.call-update) | async-done | bytes 3145744 | tf_op jit(solution)/shard_map/all_gather | solution.py:85
  331.6 10.5 %fusion.18 = f32[384,1536]{1,0:T(8,128)} fusion(f32[384,1536]{1,0:T(8,128)} %fusion, bf16[384,4096]{1,0:T(8,128)(2,1)} %all-gather.9.cloned.1.call-done, bf16[2,4096,1536]{2,1,0:T(8,128)(2,1)} %param.19), kind=kOutput, calls=%fused_computation.23 | convolution fusion | flops 4832428032 | bytes 20447232 | tf_op jit(solution)/shard_map/dot_general | solution.py:86
  342.1 31.9 %reduce-scatter.2.cloned.1.call-done = f32[96,1536]{1,0:T(8,128)} async-done(((f32[384,1536]{1,0:T(8,128)}), f32[96,1536]{1,0:T(8,128)}) %reduce-scatter.2.cloned.1.call-update) | async-done | bytes 589840 | tf_op jit(solution)/shard_map/reduce_scatter | solution.py:88
  374.0 1.8 convert_element_type.16
  (51 shorter events, 0.5 us)
Async XLA Ops:
  6.5 83.8 %copy-start = (bf16[8,2,64,1024]{3,2,1,0:T(8,128)(2,1)S(1)}, bf16[8,2,64,1024]{3,2,1,0:T(8,128)(2,1)}, u32[]{:S(2)}) copy-start(bf16[8,2,64,1024]{3,2,1,0:T(8,128)(2,1)} %param.21) | copy-start | bytes 6291460
  6.5 78.6 %copy-start.13 = (s32[3]{0:T(128)S(1)}, s32[3]{0:T(128)}, u32[]{:S(2)}) copy-start(s32[3]{0:T(128)} %param.14) | copy-start | bytes 40
  6.5 78.6 %copy-start.2 = (s32[8]{0:T(128)S(1)}, s32[8]{0:T(128)}, u32[]{:S(2)}) copy-start(s32[8]{0:T(128)} %param.15) | copy-start | bytes 100
  6.5 24.8 %all-gather.5.cloned.1.call-start = ((), (), s32[]{:S(2)}) async-start(), calls=%async_computation.1 | async-start | bytes 1966080 | tf_op jit(solution)/shard_map/all_gather | solution.py:34
  7.3 77.9 %all-gather.7.cloned.1.call-start = ((), (), s32[]{:S(2)}) async-start(), calls=%async_computation.2 | async-start | bytes 2949120 | tf_op jit(solution)/shard_map/all_gather | solution.py:38
  33.4 52.5 %copy-start.5 = (bf16[3,128,1536]{2,1,0:T(8,128)(2,1)}, bf16[3,128,1536]{2,1,0:T(8,128)(2,1)S(1)}, u32[]{:S(2)}) copy-start(bf16[3,128,1536]{2,1,0:T(8,128)(2,1)S(1)} %gather_fusion) | copy-start | bytes 3538948
  34.5 144.6 %all-reduce.2.cloned.1.call-start = ((), (), s32[]{:S(2)}) async-start(), calls=%async_computation.3 | async-start | bytes 393216 | tf_op jit(solution)/shard_map/psum | solution.py:68
  85.1 96.0 %collective-permute-start = (bf16[192,6144]{1,0:T(8,128)(2,1)}, bf16[192,6144]{1,0:T(8,128)(2,1)}, u32[]{:S(2)}, u32[]{:S(2)}) collective-permute-start(bf16[192,6144]{1,0:T(8,128)(2,1)} %all-gather.7.cloned.1.call-done), channel_id=1, source_target_pairs={{0,4},{4,0},{1,5},{5,1},{2,6},{6,2},{3,7},{7,3},{8,12},{12,8},{9,1... | collective-permute-start | bytes 7077896 | tf_op jit(solution)/shard_map/ppermute | solution.py:39
  87.6 1.3 copy-start.6
  87.8 2.5 copy-start.12
  90.2 177.7 %all-gather.11.cloned.1.call-start = ((), (), s32[]{:S(2)}) async-start(), calls=%async_computation.5 | async-start | bytes 3932160 | tf_op jit(solution)/shard_map/all_gather | solution.py:85
  180.7 2.3 copy-start.7
  181.1 13.5 %copy-start.3 = (f32[3,128,2,1024]{3,1,0,2:T(8,128)}, f32[3,128,2,1024]{3,1,0,2:T(8,128)S(1)}, u32[]{:S(2)}) copy-start(f32[3,128,2,1024]{3,1,0,2:T(8,128)S(1)} %copy.17) | copy-start | bytes 9437188
  181.1 3.9 %copy-start.14 = (bf16[6144,8]{0,1:T(8,128)(2,1)S(1)}, bf16[6144,8]{0,1:T(8,128)(2,1)}, u32[]{:S(2)}) copy-start(bf16[6144,8]{0,1:T(8,128)(2,1)} %param.16) | copy-start | bytes 294916
  185.0 9.6 %copy-start.8 = (bf16[192,6144]{1,0:T(8,128)(2,1)}, bf16[192,6144]{1,0:T(8,128)(2,1)S(1)}, u32[]{:S(2)}) copy-start(bf16[192,6144]{1,0:T(8,128)(2,1)S(1)} %get-tuple-element.15) | copy-start | bytes 7077892
  185.0 9.6 %copy-start.10 = (bf16[192,6144]{1,0:T(8,128)(2,1)}, bf16[192,6144]{1,0:T(8,128)(2,1)S(1)}, u32[]{:S(2)}) copy-start(bf16[192,6144]{1,0:T(8,128)(2,1)S(1)} %get-tuple-element.16) | copy-start | bytes 7077892
  205.4 126.2 %all-gather.9.cloned.1.call-start = ((), (), s32[]{:S(2)}) async-start(), calls=%async_computation.4 | async-start | bytes 3932160 | tf_op jit(solution)/shard_map/all_gather | solution.py:85
  205.6 9.6 %copy-start.4 = (f32[3,128,2,1024]{3,1,0,2:T(8,128)S(1)}, f32[3,128,2,1024]{3,1,0,2:T(8,128)}, u32[]{:S(2)}) copy-start(f32[3,128,2,1024]{3,1,0,2:T(8,128)} %copy-done.3) | copy-start | bytes 9437188
  205.6 9.6 %copy-start.9 = (bf16[192,6144]{1,0:T(8,128)(2,1)S(1)}, bf16[192,6144]{1,0:T(8,128)(2,1)}, u32[]{:S(2)}) copy-start(bf16[192,6144]{1,0:T(8,128)(2,1)} %copy-done.8) | copy-start | bytes 7077892
  205.6 9.6 %copy-start.11 = (bf16[192,6144]{1,0:T(8,128)(2,1)S(1)}, bf16[192,6144]{1,0:T(8,128)(2,1)}, u32[]{:S(2)}) copy-start(bf16[192,6144]{1,0:T(8,128)(2,1)} %copy-done.10) | copy-start | bytes 7077892
  226.0 148.0 %reduce-scatter.2.cloned.1.call-start = ((), (), s32[]{:S(2)}) async-start(), calls=%async_computation.6 | async-start | bytes 2949120 | tf_op jit(solution)/shard_map/reduce_scatter | solution.py:88
  331.6 44.3 %copy-start.1 = (bf16[8,2,64,1024]{3,2,1,0:T(8,128)(2,1)S(1)}, bf16[8,2,64,1024]{3,2,1,0:T(8,128)(2,1)}, u32[]{:S(2)}) copy-start(bf16[8,2,64,1024]{3,2,1,0:T(8,128)(2,1)} %param.21) | copy-start | bytes 6291460
Sparse Core Ops, SparseCore 0:
  8.9 22.3 all-gather.4
  34.6 50.4 all-gather.6
  90.4 88.7 all-reduce.1
  205.5 62.4 all-gather.10
  269.4 62.1 all-gather.8
  342.2 31.7 reduce-scatter.1
where the time goes:
time: 383 us
  waiting for transfers between devices  290 us (76%)
  matrix products  63.1 us (16%)
  between operations  13.8 us (4%)
  local copies, waits for them, and re-layouts  8.6 us (2%)
  other arithmetic  6.66 us (2%)
    all_gather x2, waiting for transfers between devices, per_device(): gathered = lax.all_gather(hidden, 'expert', axis=1, tiled=True)  95.5 us
    psum x1, waiting for transfers between devices, per_device(): lax.psum(partial_rank, GROUP)  88.2 us
    all_gather x1, waiting for transfers between devices, per_device(): mine = lax.all_gather(mine_q, 'expert', axis=1, tiled=True)  50.6 us
    reduce_scatter x1, waiting for transfers between devices, per_device(): lax.psum_scatter(running, WIDE, scatter_dimension=0, tiled=True)  31.9 us
    all_gather x1, waiting for transfers between devices, per_device(): slots_q = lax.all_gather(prompts, WIDE, axis=0, tiled=True)  23.2 us
    dot_general x2, matrix products, per_device(): jnp.dot(input_rows, up_weight[expert_number], preferred_element_type=jnp....  21.6 us
    dot_general x2, matrix products, per_device(): jnp.dot(gathered, down_weight[expert_number], preferred_element_type=jnp....  20.5 us
    dot_general x2, matrix products, per_device(): jnp.dot(input_rows, gate_weight[expert_number], preferred_element_type=jn...  17.7 us
  transfers between devices with their start and end apart: 7, of which 6 were waited for; matrix products, arithmetic and copies ran while one was open for 10% of the time, Pallas kernels for 0%

commit v1 on v0

--- a/solution.py
+++ b/solution.py
@@ -8,6 +8,11 @@
 ADAPTER_SCALE = 0.5
 WIDE = ("wy", "wc")
 GROUP = ("wy", "wc", "expert")
+
+
+def add_all(value, name):
+    terms = lax.all_gather(value, name)
+    return jnp.sum(terms, axis=0)
 
 
 def per_device(
@@ -65,7 +70,7 @@
     partial_rank = jnp.where(
         (owners == wide_index)[:, None, None, None], partial_rank, jnp.zeros_like(partial_rank)
     )
-    lowrank = lax.reduce_precision(lax.psum(partial_rank, GROUP), exponent_bits=8, mantissa_bits=7)
+    lowrank = lax.reduce_precision(add_all(partial_rank, GROUP), exponent_bits=8, mantissa_bits=7)
     tile_up = jnp.take(adapter_up_weight, tile_tenant_index, axis=0)
     adapted_hidden = jnp.einsum(
         "nter,nerf->ntef", lowrank, tile_up.astype(jnp.float32), preferred_element_type=jnp.float32

time: 383 us -> 337 us (0.88)
  waiting for transfers between devices: 290 us -> 242 us
    psum x1 -> x0, waiting for transfers between devices: 88.2 us -> none  [per_device(): lax.psum(partial_rank, GROUP)]
    all_gather x0 -> x1, waiting for transfers between devices: none -> 45.7 us  [add_all(): terms = lax.all_gather(value, name)]
    all_gather x1, waiting for transfers between devices: 50.6 us -> 45.4 us  [per_device(): mine = lax.all_gather(mine_q, 'expert', axis=1, tiled=True)]
  transfers between devices with their start and end apart: 7 -> 7, of which waited for: 6 -> 6; matrix products, arithmetic and copies ran while one was open for 10% -> 12% of each run, Pallas kernels for 0% -> 0%
where the time goes in v1:
time: 337 us; the launch traced here: 336 us
  waiting for transfers between devices  242 us (72%)
  matrix products  62.2 us (18%)
  between operations  13.8 us (4%)
  other arithmetic  8.78 us (3%)
  local copies, waits for them, and re-layouts  8.61 us (3%)
    all_gather x2, waiting for transfers between devices, per_device(): gathered = lax.all_gather(hidden, 'expert', axis=1, tiled=True)  95.3 us
    all_gather x1, waiting for transfers between devices, add_all(): terms = lax.all_gather(value, name)  45.7 us
    all_gather x1, waiting for transfers between devices, per_device(): mine = lax.all_gather(mine_q, 'expert', axis=1, tiled=True)  45.4 us
    reduce_scatter x1, waiting for transfers between devices, per_device(): lax.psum_scatter(running, WIDE, scatter_dimension=0, tiled=True)  31.9 us
    all_gather x1, waiting for transfers between devices, per_device(): slots_q = lax.all_gather(prompts, WIDE, axis=0, tiled=True)  23.2 us
    dot_general x2, matrix products, per_device(): jnp.dot(input_rows, up_weight[expert_number], preferred_element_type=jnp....  21.6 us
    dot_general x2, matrix products, per_device(): jnp.dot(gathered, down_weight[expert_number], preferred_element_type=jnp....  20.5 us
    dot_general x2, matrix products, per_device(): jnp.dot(input_rows, gate_weight[expert_number], preferred_element_type=jn...  17.7 us
  transfers between devices with their start and end apart: 7, of which 6 were waited for; matrix products, arithmetic and copies ran while one was open for 12% of the time, Pallas kernels for 0%

profile of v1, /device:TPU:0, one launch (start us, length us, event | category | flops | bytes accessed | tf_op | source)
XLA Modules:
  0.0 336.1 jit_solution(3860571992430907327)
XLA Ops:
  6.5 0.7 all-gather.7.cloned.1.call-update
  7.3 0.7 compare_and_fusion.2
  8.1 0.1 dynamic-slice
  8.1 23.2 %all-gather.7.cloned.1.call-done = bf16[4,128,1536]{2,1,0:T(8,128)(2,1)} async-done(((bf16[1,128,1536]{2,1,0:T(8,128)(2,1)}), bf16[4,128,1536]{2,1,0:T(8,128)(2,1)}) %all-gather.7.cloned.1.call-update) | async-done | bytes 1572880 | tf_op jit(solution)/shard_map/all_gather | solution.py:39
  31.3 2.0 gather_fusion
  33.4 1.2 dynamic-slice_select_fusion
  34.7 0.6 gather_fusion.2
  35.4 1.8 gather_fusion.3
  37.1 0.2 broadcast_select_fusion.2
  37.3 1.1 copy-done.6
  38.4 0.5 fusion.33
  38.9 0.8 broadcast_select_fusion.3
  39.8 45.4 %all-gather.9.cloned.1.call-done = bf16[192,6144]{1,0:T(8,128)(2,1)} async-done(((bf16[192,1536]{1,0:T(8,128)(2,1)}), bf16[192,6144]{1,0:T(8,128)(2,1)}) %all-gather.9.cloned.1.call-update) | async-done | bytes 2359312 | tf_op jit(solution)/shard_map/all_gather | solution.py:43
  85.2 0.6 gather_fusion.1
  85.8 45.7 %all-gather.15.cloned.1.call-done = f32[48,128,2,64]{1,3,2,0:T(8,128)} async-done(((f32[3,128,2,64]{1,3,2,0:T(8,128)}), f32[48,128,2,64]{1,3,2,0:T(8,128)}) %all-gather.15.cloned.1.call-update) | async-done | bytes 3145744 | tf_op jit(solution)/shard_map/all_gather | solution.py:14
  131.5 2.1 reduce_sum.19
  133.6 0.6 convolution_bitcast_fusion
  134.3 0.4 copy.17
  134.7 1.9 copy-done.7
  136.6 2.0 broadcast_select_fusion.1
  138.6 1.3 fusion.48
  140.0 8.1 %fusion.4 = f32[384,1024]{1,0:T(8,128)S(1)} fusion(bf16[2,6144,1024]{2,1,0:T(8,128)(2,1)} %param.17, bf16[192,6144]{1,0:T(8,128)(2,1)S(1)} %get-tuple-element.16, bf16[192,6144]{1,0:T(8,128)(2,1)S(1)} %get-tuple-element.15), kind=kOutput, calls=%fused_computation.8 | convolution fusion | flops 4841275392 | bytes 18874368 | tf_op jit(solution)/shard_map/dot_general | solution.py:80
  148.2 10.7 %fusion.24 = bf16[384,1024]{1,0:T(8,128)(2,1)} fusion(f32[384,2,1024]{2,0,1:T(8,128)S(1)} %bitcast.67, f32[384,1024]{1,0:T(8,128)S(1)} %fusion.4, bf16[2,6144,1024]{2,1,0:T(8,128)(2,1)} %param.18, f32[384]{0:T(512)S(1)} %get-tuple-element.6, bf16[192,6144]{1,0:T(8,128)(2,1)S(1)} %get-tuple-element.16, bf16[192,6144]{1,0:T(8,128)(2,1)S(1)} %get-tuple-element.15), kind=kOutput, calls=%fused_computation.31 | convolution fusion | flops 4844814336 | bytes 21235200 | tf_op jit(solution)/shard_map/dot_general | solution.py:84
  158.9 0.2 all-gather.11.cloned.1.call-start
  159.2 9.5 %fusion.10 = f32[384,1024]{1,0:T(8,128)S(1)} fusion(bf16[2,6144,1024]{2,1,0:T(8,128)(2,1)} %param.17, bf16[192,6144]{1,0:T(8,128)(2,1)} %copy-done.10, bf16[192,6144]{1,0:T(8,128)(2,1)} %copy-done.8), kind=kOutput, calls=%fused_computation.14 | convolution fusion | flops 4841275392 | bytes 18874368 | tf_op jit(solution)/shard_map/dot_general | solution.py:80
  168.8 10.8 %fusion.28 = bf16[384,1024]{1,0:T(8,128)(2,1)} fusion(f32[384,2,1024]{2,0,1:T(8,128)S(1)} %bitcast.68, f32[384,1024]{1,0:T(8,128)S(1)} %fusion.10, bf16[2,6144,1024]{2,1,0:T(8,128)(2,1)} %param.18, f32[384]{0:T(512)S(1)} %get-tuple-element.5, bf16[192,6144]{1,0:T(8,128)(2,1)S(1)} %copy-done.11, bf16[192,6144]{1,0:T(8,128)(2,1)S(1)} %copy-done.9), kind=kOutput, calls=%fused_computation.36 | convolution fusion | flops 4844814336 | bytes 21235200 | tf_op jit(solution)/shard_map/dot_general | solution.py:84
  179.7 41.7 %all-gather.13.cloned.1.call-done = bf16[384,4096]{1,0:T(8,128)(2,1)} async-done(((bf16[384,1024]{1,0:T(8,128)(2,1)}), bf16[384,4096]{1,0:T(8,128)(2,1)}) %all-gather.13.cloned.1.call-update) | async-done | bytes 3145744 | tf_op jit(solution)/shard_map/all_gather | solution.py:90
  221.4 10.0 %fusion = f32[384,1536]{1,0:T(8,128)} fusion(bf16[384,4096]{1,0:T(8,128)(2,1)} %all-gather.13.cloned.1.call-done, bf16[2,4096,1536]{2,1,0:T(8,128)(2,1)} %param.19), kind=kOutput, calls=%fused_computation.4 | convolution fusion | flops 4831838208 | bytes 18087936 | tf_op jit(solution)/shard_map/dot_general | solution.py:91
  231.4 53.6 %all-gather.11.cloned.1.call-done = bf16[384,4096]{1,0:T(8,128)(2,1)} async-done(((bf16[384,1024]{1,0:T(8,128)(2,1)}), bf16[384,4096]{1,0:T(8,128)(2,1)}) %all-gather.11.cloned.1.call-update) | async-done | bytes 3145744 | tf_op jit(solution)/shard_map/all_gather | solution.py:90
  285.0 10.5 %fusion.18 = f32[384,1536]{1,0:T(8,128)} fusion(f32[384,1536]{1,0:T(8,128)} %fusion, bf16[384,4096]{1,0:T(8,128)(2,1)} %all-gather.11.cloned.1.call-done, bf16[2,4096,1536]{2,1,0:T(8,128)(2,1)} %param.19), kind=kOutput, calls=%fused_computation.23 | convolution fusion | flops 4832428032 | bytes 20447232 | tf_op jit(solution)/shard_map/dot_general | solution.py:91
  295.5 31.9 %reduce-scatter.2.cloned.1.call-done = f32[96,1536]{1,0:T(8,128)} async-done(((f32[384,1536]{1,0:T(8,128)}), f32[96,1536]{1,0:T(8,128)}) %reduce-scatter.2.cloned.1.call-update) | async-done | bytes 589840 | tf_op jit(solution)/shard_map/reduce_scatter | solution.py:93
  327.4 1.8 convert_element_type.16
  (52 shorter events, 0.6 us)
Async XLA Ops:
  6.5 78.6 %copy-start = (bf16[8,2,64,1024]{3,2,1,0:T(8,128)(2,1)S(1)}, bf16[8,2,64,1024]{3,2,1,0:T(8,128)(2,1)}, u32[]{:S(2)}) copy-start(bf16[8,2,64,1024]{3,2,1,0:T(8,128)(2,1)} %param.21) | copy-start | bytes 6291460
  6.5 28.1 %copy-start.13 = (s32[3]{0:T(128)S(1)}, s32[3]{0:T(128)}, u32[]{:S(2)}) copy-start(s32[3]{0:T(128)} %param.14) | copy-start | bytes 40
  6.5 28.1 %copy-start.2 = (s32[8]{0:T(128)S(1)}, s32[8]{0:T(128)}, u32[]{:S(2)}) copy-start(s32[8]{0:T(128)} %param.15) | copy-start | bytes 100
  6.5 24.8 %all-gather.7.cloned.1.call-start = ((), (), s32[]{:S(2)}) async-start(), calls=%async_computation.1 | async-start | bytes 1966080 | tf_op jit(solution)/shard_map/all_gather | solution.py:39
  7.3 77.9 %all-gather.9.cloned.1.call-start = ((), (), s32[]{:S(2)}) async-start(), calls=%async_computation.2 | async-start | bytes 2949120 | tf_op jit(solution)/shard_map/all_gather | solution.py:43
  33.4 2.0 copy-start.5
  34.6 97.0 %all-gather.15.cloned.1.call-start = ((), (), s32[]{:S(2)}) async-start(), calls=%async_computation.6 | async-start | bytes 3342336 | tf_op jit(solution)/shard_map/all_gather | solution.py:14
  37.1 1.3 copy-start.6
  38.4 47.4 %copy-start.12 = (s32[384,2]{0,1:T(2,128)S(1)}, s32[384,2]{0,1:T(2,128)}, u32[]{:S(2)}) copy-start(s32[384,2]{0,1:T(2,128)} %param.13) | copy-start | bytes 9220
  39.7 181.6 %all-gather.13.cloned.1.call-start = ((), (), s32[]{:S(2)}) async-start(), calls=%async_computation.4 | async-start | bytes 3932160 | tf_op jit(solution)/shard_map/all_gather | solution.py:90
  85.2 49.5 %collective-permute-start = (bf16[192,6144]{1,0:T(8,128)(2,1)}, bf16[192,6144]{1,0:T(8,128)(2,1)}, u32[]{:S(2)}, u32[]{:S(2)}) collective-permute-start(bf16[192,6144]{1,0:T(8,128)(2,1)} %all-gather.9.cloned.1.call-done), channel_id=1, source_target_pairs={{0,4},{4,0},{1,5},{5,1},{2,6},{6,2},{3,7},{7,3},{8,12},{12,8},{9,1... | collective-permute-start | bytes 7077896 | tf_op jit(solution)/shard_map/ppermute | solution.py:44
  134.3 2.3 copy-start.7
  134.7 13.5 %copy-start.3 = (f32[3,128,2,1024]{3,1,0,2:T(8,128)}, f32[3,128,2,1024]{3,1,0,2:T(8,128)S(1)}, u32[]{:S(2)}) copy-start(f32[3,128,2,1024]{3,1,0,2:T(8,128)S(1)} %copy.17) | copy-start | bytes 9437188
  134.7 3.9 %copy-start.14 = (bf16[6144,8]{0,1:T(8,128)(2,1)S(1)}, bf16[6144,8]{0,1:T(8,128)(2,1)}, u32[]{:S(2)}) copy-start(bf16[6144,8]{0,1:T(8,128)(2,1)} %param.16) | copy-start | bytes 294916
  138.6 9.6 %copy-start.8 = (bf16[192,6144]{1,0:T(8,128)(2,1)}, bf16[192,6144]{1,0:T(8,128)(2,1)S(1)}, u32[]{:S(2)}) copy-start(bf16[192,6144]{1,0:T(8,128)(2,1)S(1)} %get-tuple-element.15) | copy-start | bytes 7077892
  138.6 9.6 %copy-start.10 = (bf16[192,6144]{1,0:T(8,128)(2,1)}, bf16[192,6144]{1,0:T(8,128)(2,1)S(1)}, u32[]{:S(2)}) copy-start(bf16[192,6144]{1,0:T(8,128)(2,1)S(1)} %get-tuple-element.16) | copy-start | bytes 7077892
  158.9 126.0 %all-gather.11.cloned.1.call-start = ((), (), s32[]{:S(2)}) async-start(), calls=%async_computation.3 | async-start | bytes 3932160 | tf_op jit(solution)/shard_map/all_gather | solution.py:90
  159.2 9.6 %copy-start.4 = (f32[3,128,2,1024]{3,1,0,2:T(8,128)S(1)}, f32[3,128,2,1024]{3,1,0,2:T(8,128)}, u32[]{:S(2)}) copy-start(f32[3,128,2,1024]{3,1,0,2:T(8,128)} %copy-done.3) | copy-start | bytes 9437188
  159.2 9.6 %copy-start.9 = (bf16[192,6144]{1,0:T(8,128)(2,1)S(1)}, bf16[192,6144]{1,0:T(8,128)(2,1)}, u32[]{:S(2)}) copy-start(bf16[192,6144]{1,0:T(8,128)(2,1)} %copy-done.8) | copy-start | bytes 7077892
  159.2 9.6 %copy-start.11 = (bf16[192,6144]{1,0:T(8,128)(2,1)S(1)}, bf16[192,6144]{1,0:T(8,128)(2,1)}, u32[]{:S(2)}) copy-start(bf16[192,6144]{1,0:T(8,128)(2,1)} %copy-done.10) | copy-start | bytes 7077892
  179.6 147.8 %reduce-scatter.2.cloned.1.call-start = ((), (), s32[]{:S(2)}) async-start(), calls=%async_computation.5 | async-start | bytes 2949120 | tf_op jit(solution)/shard_map/reduce_scatter | solution.py:93
  285.0 44.2 %copy-start.1 = (bf16[8,2,64,1024]{3,2,1,0:T(8,128)(2,1)S(1)}, bf16[8,2,64,1024]{3,2,1,0:T(8,128)(2,1)}, u32[]{:S(2)}) copy-start(bf16[8,2,64,1024]{3,2,1,0:T(8,128)(2,1)} %param.21) | copy-start | bytes 6291460
Sparse Core Ops, SparseCore 0:
  8.9 22.3 all-gather.6
  34.7 50.4 all-gather.8
  87.5 44.0 all-gather.14
  159.1 62.2 all-gather.12
  222.8 62.1 all-gather.10
  295.6 31.7 reduce-scatter.1
